TPU v7x, 512 devices: a whole 4x4x16 slice. The times are simulated.
512 devices in a mesh: patch: 16 (over y, x_hi, core), map: 32 (over x_lo, z).
Axes of the slice: x: 4 (x_hi: 2, x_lo: 2; x = x_hi * 2 + x_lo), y: 4, z: 16, core: 2. Of those that a mesh axis runs over, the one named last changes fastest.
Arguments:
- maps: bfloat16 [64, 32, 24576], P('map', None, 'patch'), may hold values from -6 to 6
- cotangent: bfloat16 [64, 32, 24576], P('map', None, 'patch'), may hold values from -6 to 6
- tiles: bfloat16 [96, 3, 256, 256], P('patch'), may hold values from -0.21875 to 0.21875
- columns: int32 [96, 3], P('patch'), may hold values from 0 to 95, as said below
- filters: bfloat16 [3, 32, 32], replicated, may hold values from -0.625 to 0.625
Outputs:
- output: bfloat16 [64, 32, 24576], P('map', None, 'patch')
- input_grad: bfloat16 [64, 32, 24576], P('map', None, 'patch')
- filter_grad: float32 [3, 32, 32], replicated
Inputs may be any that keep to these rules, and one draw needn't show every extreme that they name: `columns`: slot 0 of block row b names block b itself, slot 1 a block 1 to 2 before it and slot 2 a block 1 to 2 after it, counted cyclically over the 96 blocks; block row 0 reads exactly 2 blocks away on both sides.
All inputs are finite; a program needn't handle non-finite values.
Results may differ from a plain program's by a relative error of at most 0.0054.
Values may be sent and summed in bfloat16 or wider, within the bound.
No kernel may reach another device: no remote copies, remote signals or barrier semaphores. Data moves between devices by JAX's collectives and lax.ppermute only.
A program may use at most 64 MiB of HBM per device.

v0:
```python
import math
import jax
import jax.numpy as jnp
from jax import lax
from jax.sharding import PartitionSpec as P

REACH = 2


def extended_2(cells, sides, width):
    for axis, dim in sides:
        count = lax.axis_size(axis)
        head = lax.slice_in_dim(cells, 0, width, axis=dim)
        tail = lax.slice_in_dim(cells, cells.shape[dim] - width, cells.shape[dim], axis=dim)
        cells = jnp.concatenate(
            [
                lax.ppermute(tail, axis, [(i, (i + 1) % count) for i in range(count)]),
                cells,
                lax.ppermute(head, axis, [((i + 1) % count, i) for i in range(count)]),
            ],
            axis=dim,
        )
    return cells


def offset_sums(grad_blocks, tile_set, offset_mask):
    contrib = jnp.einsum(
        "nui,ujiq->nujq", grad_blocks, tile_set, preferred_element_type=jnp.float32
    )
    return jnp.einsum(
        "uje,nujq->nueq", offset_mask.astype(jnp.float32), contrib, precision=lax.Precision.HIGHEST
    )


def per_device(maps, cotangent, tiles, columns, filters):
    map_count = maps.shape[0]
    chan_count = maps.shape[1]
    pix_count = maps.shape[2]
    block_count = tiles.shape[0]
    block_size = tiles.shape[2]
    reach_blocks = REACH
    spread = 2 * reach_blocks + 1
    row_count = map_count * chan_count
    rim_cells = reach_blocks * block_size
    patch_count = lax.axis_size("patch")
    total_blocks = block_count * patch_count
    first_block = lax.axis_index("patch") * block_count
    row_ids = first_block + jnp.arange(block_count, dtype=jnp.int32)
    offset_ids = jnp.arange(spread, dtype=jnp.int32)
    own_offset = (columns - row_ids[:, None] + reach_blocks) % total_blocks
    own_mask = own_offset[:, :, None] == offset_ids[None, None, :]

    def forward_apply(field):
        extended = extended_2(field, (("patch", 2),), rim_cells)
        ext_blocks = extended.reshape(row_count, block_count + 2 * reach_blocks, block_size)
        shifted = jnp.stack(
            [ext_blocks[:, offset : offset + block_count] for offset in range(spread)], axis=2
        )
        picked = jnp.einsum(
            "rje,nreq->nrjq",
            own_mask.astype(jnp.bfloat16),
            shifted,
            preferred_element_type=jnp.bfloat16,
        )
        result = jnp.einsum("nrjq,rjiq->nri", picked, tiles, preferred_element_type=jnp.float32)
        return result.reshape(map_count, chan_count, pix_count)

    def adjoint_apply(grads):
        by_offset = offset_sums(grads.reshape(row_count, block_count, block_size), tiles, own_mask)
        window = jnp.pad(by_offset[:, :, 0], ((0, 0), (0, spread - 1), (0, 0)))
        for offset in range(1, spread):
            window = window + jnp.pad(
                by_offset[:, :, offset], ((0, 0), (offset, spread - 1 - offset), (0, 0))
            )
        own_part = window[:, reach_blocks : reach_blocks + block_count]
        outgoing = jnp.concatenate(
            [window[:, :reach_blocks], window[:, reach_blocks + block_count :]], axis=1
        )
        outgoing = outgoing.reshape(map_count, chan_count, 2 * rim_cells)
        incoming = extended_2(outgoing, (("patch", 2),), rim_cells)
        from_left = incoming[:, :, :rim_cells].reshape(row_count, reach_blocks, block_size)
        from_right = incoming[:, :, incoming.shape[2] - rim_cells :].reshape(
            row_count, reach_blocks, block_size
        )
        own_part = own_part.at[:, :reach_blocks].add(from_left)
        own_part = own_part.at[:, block_count - reach_blocks :].add(from_right)
        return own_part.reshape(map_count, chan_count, pix_count)

    x_one = forward_apply(maps).astype(jnp.bfloat16)
    x_two = (2.0 * forward_apply(x_one) - maps.astype(jnp.float32)).astype(jnp.bfloat16)
    terms = jnp.stack([maps, x_one, x_two])
    output = jnp.einsum("kco,kmcp->mop", filters, terms, preferred_element_type=jnp.float32).astype(
        jnp.bfloat16
    )
    grads = jnp.einsum("kco,mop->kmcp", filters, cotangent, preferred_element_type=jnp.float32)
    grad_two = grads[2].astype(jnp.bfloat16)
    update = (grads[1] + 2.0 * adjoint_apply(grad_two)).astype(jnp.bfloat16)
    input_grad = (grads[0] - grad_two.astype(jnp.float32) + adjoint_apply(update)).astype(
        jnp.bfloat16
    )
    scale = 1.0 / math.sqrt(map_count * lax.axis_size("map") * pix_count * patch_count)
    local_grad = jnp.einsum("kmcp,mop->kco", terms, cotangent, preferred_element_type=jnp.float32)
    filter_grad = lax.psum(local_grad, ("patch", "map")) * scale
    return (output, input_grad, filter_grad)


def solution(mesh):
    placed = (
        P("map", None, "patch"),
        P("map", None, "patch"),
        P("patch", None, None, None),
        P("patch", None),
        P(),
    )
    return jax.shard_map(
        per_device,
        mesh=mesh,
        in_specs=placed,
        out_specs=(P("map", None, "patch"), P("map", None, "patch"), P()),
        check_vma=False,
    )
```

profile of v0, /device:TPU:1, one launch (start us, length us, event | category | flops | bytes accessed | tf_op | source)
XLA Modules:
  0.0 221.6 jit_solution(9846326644404595408)
XLA Ops:
  4.6 2.3 %convolution_bitcast_fusion.3 = f32[64,6,5,256]{3,2,0,1:T(8,128)S(1)} fusion(f32[6,64,3,256]{3,1,2,0:T(8,128)S(1)} %fusion.38, s32[6,3]{1,0:T(8,128)S(1)} %copy.21), kind=kOutput, calls=%fused_computation.5 | convolution fusion | flops 17694810 | bytes 3145800 | tf_op jit(solution)/shard_map/uje,nujq->nueq/dot_general | solution.py:30
  6.9 1.8 fusion.56
  10.8 1.8 reshape.181
  12.6 1.8 fusion.58
  14.4 6.0 %collective-permute-start.4 = (f32[2,32,512]{2,1,0:T(8,128)}, f32[2,32,512]{2,1,0:T(8,128)}, u32[]{:S(2)}, u32[]{:S(2)}) collective-permute-start(f32[2,32,512]{2,1,0:T(8,128)} %get-tuple-element.68), channel_id=1, source_target_pairs={{0,32},{32,64},{64,96},{96,128},{128,160},{160,192},{192,224},{224... | collective-permute-start | bytes 393224 | tf_op jit(solution)/shard_map/ppermute | solution.py:17
  20.4 4.7 %collective-permute-start.5 = (f32[2,32,512]{2,1,0:T(8,128)}, f32[2,32,512]{2,1,0:T(8,128)}, u32[]{:S(2)}, u32[]{:S(2)}) collective-permute-start(f32[2,32,512]{2,1,0:T(8,128)} %get-tuple-element.67), channel_id=1, source_target_pairs={{32,0},{64,32},{96,64},{128,96},{160,128},{192,160},{224,192},{256... | collective-permute-start | bytes 393224 | tf_op jit(solution)/shard_map/ppermute | solution.py:19
  26.6 2.4 %collective-permute-start = (bf16[2,32,512]{2,1,0:T(8,128)(2,1)}, bf16[2,32,512]{2,1,0:T(8,128)(2,1)}, u32[]{:S(2)}, u32[]{:S(2)}) collective-permute-start(bf16[2,32,512]{2,1,0:T(8,128)(2,1)} %get-tuple-element.71), channel_id=1, source_target_pairs={{0,32},{32,64},{64,96},{96,128},{128,160},{160,192},{192,224},{224... | collective-permute-start | bytes 196616 | tf_op jit(solution)/shard_map/ppermute | solution.py:17
  29.0 6.8 %collective-permute-start.1 = (bf16[2,32,512]{2,1,0:T(8,128)(2,1)}, bf16[2,32,512]{2,1,0:T(8,128)(2,1)}, u32[]{:S(2)}, u32[]{:S(2)}) collective-permute-start(bf16[2,32,512]{2,1,0:T(8,128)(2,1)} %get-tuple-element.72), channel_id=1, source_target_pairs={{32,0},{64,32},{96,64},{128,96},{160,128},{192,160},{224,192},{256... | collective-permute-start | bytes 196616 | tf_op jit(solution)/shard_map/ppermute | solution.py:19
  35.8 1.8 slice.264
  38.5 1.9 squeeze.35
  46.6 1.9 convert_element_type.73
  48.4 1.9 convert_element_type.72
  51.8 1.9 collective-permute-start.2
  53.7 7.4 %collective-permute-start.3 = (bf16[2,32,512]{2,1,0:T(8,128)(2,1)}, bf16[2,32,512]{2,1,0:T(8,128)(2,1)}, u32[]{:S(2)}, u32[]{:S(2)}) collective-permute-start(bf16[2,32,512]{2,1,0:T(8,128)(2,1)} %get-tuple-element.70), channel_id=1, source_target_pairs={{32,0},{64,32},{96,64},{128,96},{160,128},{192,160},{224,192},{256... | collective-permute-start | bytes 196616 | tf_op jit(solution)/shard_map/ppermute | solution.py:19
  61.2 1.6 reshape.182
  62.8 1.7 fusion.44
  67.1 1.6 fusion.34
  68.7 2.3 %convolution_bitcast_fusion.2 = f32[64,6,5,256]{3,2,0,1:T(8,128)S(1)} fusion(f32[6,64,3,256]{3,1,2,0:T(8,128)S(1)} %fusion.34, s32[6,3]{1,0:T(8,128)S(1)} %copy.21), kind=kOutput, calls=%fused_computation.4 | convolution fusion | flops 17694810 | bytes 3145800 | tf_op jit(solution)/shard_map/uje,nujq->nueq/dot_general | solution.py:30
  71.0 1.8 fusion.55
  82.8 2.0 convolution_bitcast_fusion.6
  86.7 1.8 reshape.184
  88.4 1.7 fusion.57
  90.1 1.9 collective-permute-start.6
  92.0 1.8 slice.279
  93.8 7.2 %collective-permute-start.7 = (f32[2,32,512]{2,1,0:T(8,128)}, f32[2,32,512]{2,1,0:T(8,128)}, u32[]{:S(2)}, u32[]{:S(2)}) collective-permute-start(f32[2,32,512]{2,1,0:T(8,128)} %get-tuple-element.65), channel_id=1, source_target_pairs={{32,0},{64,32},{96,64},{128,96},{160,128},{192,160},{224,192},{256... | collective-permute-start | bytes 393224 | tf_op jit(solution)/shard_map/ppermute | solution.py:19
  101.0 106.8 %psum.7 = f32[3,32,32]{2,1,0:T(8,128)} all-reduce(f32[3,32,32]{2,1,0:T(8,128)} %convolution_bitcast_fusion.6), channel_id=1, replica_groups=mesh['patch'=16,'map'=32] {'patch','map'}, use_global_device_ids=true, to_apply=%region_0.1 | all-reduce | flops 3072 | bytes 24576 | tf_op jit(solution)/shard_map/psum | solution.py:103
  209.2 1.6 reshape.185
  210.9 1.7 fusion.42
  212.5 1.7 reshape.186
  215.9 2.0 copy.42
  218.0 1.9 reshape.187
  219.9 1.7 fusion.20
  (109 shorter events, 33.2 us)
Async XLA Ops:
  0.6 3.5 %copy-start = (bf16[6,3,256,256]{3,2,1,0:T(8,128)(2,1)S(1)}, bf16[6,3,256,256]{3,2,1,0:T(8,128)(2,1)}, u32[]{:S(2)}) copy-start(bf16[6,3,256,256]{3,2,1,0:T(8,128)(2,1)} %param.15) | copy-start | bytes 7077892
  2.8 1.0 copy-start.15
  8.9 28.7 %copy-start.7 = (f32[64,6,256]{2,0,1:T(8,128)}, f32[64,6,256]{2,0,1:T(8,128)S(1)}, u32[]{:S(2)}) copy-start(f32[64,6,256]{2,0,1:T(8,128)S(1)} %get-tuple-element.73) | copy-start | bytes 1179652
  8.9 28.7 %copy-start.9 = (f32[64,6,256]{2,0,1:T(8,128)}, f32[64,6,256]{2,0,1:T(8,128)S(1)}, u32[]{:S(2)}) copy-start(f32[64,6,256]{2,0,1:T(8,128)S(1)} %get-tuple-element.74) | copy-start | bytes 1179652
  9.0 0.8 copy-start.11
  9.0 1.0 copy-start.13
  12.6 25.0 %copy-start.12 = (f32[64,6,256]{2,0,1:T(8,128)S(1)}, f32[64,6,256]{2,0,1:T(8,128)}, u32[]{:S(2)}) copy-start(f32[64,6,256]{2,0,1:T(8,128)} %copy-done.11) | copy-start | bytes 1179652
  12.6 25.0 %copy-start.14 = (f32[64,6,256]{2,0,1:T(8,128)S(1)}, f32[64,6,256]{2,0,1:T(8,128)}, u32[]{:S(2)}) copy-start(f32[64,6,256]{2,0,1:T(8,128)} %copy-done.13) | copy-start | bytes 1179652
  14.4 46.8 %collective-permute-start.4 = (f32[2,32,512]{2,1,0:T(8,128)}, f32[2,32,512]{2,1,0:T(8,128)}, u32[]{:S(2)}, u32[]{:S(2)}) collective-permute-start(f32[2,32,512]{2,1,0:T(8,128)} %get-tuple-element.68), channel_id=1, source_target_pairs={{0,32},{32,64},{64,96},{96,128},{128,160},{160,192},{192,224},{224... | collective-permute-start | bytes 393224 | tf_op jit(solution)/shard_map/ppermute | solution.py:17
  20.4 44.1 %collective-permute-start.5 = (f32[2,32,512]{2,1,0:T(8,128)}, f32[2,32,512]{2,1,0:T(8,128)}, u32[]{:S(2)}, u32[]{:S(2)}) collective-permute-start(f32[2,32,512]{2,1,0:T(8,128)} %get-tuple-element.67), channel_id=1, source_target_pairs={{32,0},{64,32},{96,64},{128,96},{160,128},{192,160},{224,192},{256... | collective-permute-start | bytes 393224 | tf_op jit(solution)/shard_map/ppermute | solution.py:19
  26.6 13.8 %collective-permute-start = (bf16[2,32,512]{2,1,0:T(8,128)(2,1)}, bf16[2,32,512]{2,1,0:T(8,128)(2,1)}, u32[]{:S(2)}, u32[]{:S(2)}) collective-permute-start(bf16[2,32,512]{2,1,0:T(8,128)(2,1)} %get-tuple-element.71), channel_id=1, source_target_pairs={{0,32},{32,64},{64,96},{96,128},{128,160},{160,192},{192,224},{224... | collective-permute-start | bytes 196616 | tf_op jit(solution)/shard_map/ppermute | solution.py:17
  29.0 11.4 %collective-permute-start.1 = (bf16[2,32,512]{2,1,0:T(8,128)(2,1)}, bf16[2,32,512]{2,1,0:T(8,128)(2,1)}, u32[]{:S(2)}, u32[]{:S(2)}) collective-permute-start(bf16[2,32,512]{2,1,0:T(8,128)(2,1)} %get-tuple-element.72), channel_id=1, source_target_pairs={{32,0},{64,32},{96,64},{128,96},{160,128},{192,160},{224,192},{256... | collective-permute-start | bytes 196616 | tf_op jit(solution)/shard_map/ppermute | solution.py:19
  37.7 2.7 %copy-start.18 = (bf16[2,32,1536]{2,1,0:T(8,128)(2,1)S(1)}, bf16[2,32,1536]{2,1,0:T(8,128)(2,1)}, u32[]{:S(2)}) copy-start(bf16[2,32,1536]{2,1,0:T(8,128)(2,1)} %param.13) | copy-start | bytes 589828
  45.7 17.1 %copy-start.8 = (f32[64,6,256]{2,0,1:T(8,128)S(1)}, f32[64,6,256]{2,0,1:T(8,128)}, u32[]{:S(2)}) copy-start(f32[64,6,256]{2,0,1:T(8,128)} %copy-done.7) | copy-start | bytes 1179652
  45.7 17.1 %copy-start.10 = (f32[64,6,256]{2,0,1:T(8,128)S(1)}, f32[64,6,256]{2,0,1:T(8,128)}, u32[]{:S(2)}) copy-start(f32[64,6,256]{2,0,1:T(8,128)} %copy-done.9) | copy-start | bytes 1179652
  51.8 23.2 %collective-permute-start.2 = (bf16[2,32,512]{2,1,0:T(8,128)(2,1)}, bf16[2,32,512]{2,1,0:T(8,128)(2,1)}, u32[]{:S(2)}, u32[]{:S(2)}) collective-permute-start(bf16[2,32,512]{2,1,0:T(8,128)(2,1)} %get-tuple-element.69), channel_id=1, source_target_pairs={{0,32},{32,64},{64,96},{96,128},{128,160},{160,192},{192,224},{224... | collective-permute-start | bytes 196616 | tf_op jit(solution)/shard_map/ppermute | solution.py:17
  53.7 21.3 %collective-permute-start.3 = (bf16[2,32,512]{2,1,0:T(8,128)(2,1)}, bf16[2,32,512]{2,1,0:T(8,128)(2,1)}, u32[]{:S(2)}, u32[]{:S(2)}) collective-permute-start(bf16[2,32,512]{2,1,0:T(8,128)(2,1)} %get-tuple-element.70), channel_id=1, source_target_pairs={{32,0},{64,32},{96,64},{128,96},{160,128},{192,160},{224,192},{256... | collective-permute-start | bytes 196616 | tf_op jit(solution)/shard_map/ppermute | solution.py:19
  72.9 1.3 copy-start.1
  73.0 1.3 copy-start.3
  73.0 1.3 copy-start.5
  73.0 1.2 copy-start.6
  74.3 1.0 copy-start.17
  80.6 1.1 copy-start.19
  81.7 3.1 %copy-start.22 = (bf16[1,2,32,1536]{3,2,1,0:T(8,128)(2,1)S(1)}, bf16[1,2,32,1536]{3,2,1,0:T(8,128)(2,1)}, u32[]{:S(2)}) copy-start(bf16[1,2,32,1536]{3,2,1,0:T(8,128)(2,1)} %convert_element_type.72) | copy-start | bytes 589828
  81.7 3.1 %copy-start.23 = (bf16[3,32,32]{2,1,0:T(8,128)(2,1)S(1)}, bf16[3,32,32]{2,1,0:T(8,128)(2,1)}, u32[]{:S(2)}) copy-start(bf16[3,32,32]{2,1,0:T(8,128)(2,1)} %param.17) | copy-start | bytes 18436
  82.8 3.0 %copy-start.20 = (f32[64,2,256]{2,0,1:T(8,128)S(1)}, f32[64,2,256]{2,0,1:T(8,128)}, u32[]{:S(2)}) copy-start(f32[64,2,256]{2,0,1:T(8,128)} %get-tuple-element.61) | copy-start | bytes 393220
  82.8 3.0 %copy-start.21 = (f32[64,2,256]{2,0,1:T(8,128)S(1)}, f32[64,2,256]{2,0,1:T(8,128)}, u32[]{:S(2)}) copy-start(f32[64,2,256]{2,0,1:T(8,128)} %get-tuple-element.62) | copy-start | bytes 393220
  85.8 125.1 %copy-start.2 = (f32[64,6,1,256]{3,0,1,2:T(8,128)S(1)}, f32[64,6,1,256]{3,0,1,2:T(8,128)}, u32[]{:S(2)}) copy-start(f32[64,6,1,256]{3,0,1,2:T(8,128)} %copy-done.1) | copy-start | bytes 1179652
  85.8 125.1 %copy-start.4 = (f32[64,6,1,256]{3,0,1,2:T(8,128)S(1)}, f32[64,6,1,256]{3,0,1,2:T(8,128)}, u32[]{:S(2)}) copy-start(f32[64,6,1,256]{3,0,1,2:T(8,128)} %copy-done.3) | copy-start | bytes 1179652
  90.1 119.1 %collective-permute-start.6 = (f32[2,32,512]{2,1,0:T(8,128)}, f32[2,32,512]{2,1,0:T(8,128)}, u32[]{:S(2)}, u32[]{:S(2)}) collective-permute-start(f32[2,32,512]{2,1,0:T(8,128)} %get-tuple-element.66), channel_id=1, source_target_pairs={{0,32},{32,64},{64,96},{96,128},{128,160},{160,192},{192,224},{224... | collective-permute-start | bytes 393224 | tf_op jit(solution)/shard_map/ppermute | solution.py:17
  93.8 118.8 %collective-permute-start.7 = (f32[2,32,512]{2,1,0:T(8,128)}, f32[2,32,512]{2,1,0:T(8,128)}, u32[]{:S(2)}, u32[]{:S(2)}) collective-permute-start(f32[2,32,512]{2,1,0:T(8,128)} %get-tuple-element.65), channel_id=1, source_target_pairs={{32,0},{64,32},{96,64},{128,96},{160,128},{192,160},{224,192},{256... | collective-permute-start | bytes 393224 | tf_op jit(solution)/shard_map/ppermute | solution.py:19
  212.5 7.3 %copy-start.16 = (f32[3,2,32,1536]{3,2,0,1:T(8,128)S(1)}, f32[3,2,32,1536]{3,2,0,1:T(8,128)}, u32[]{:S(2)}) copy-start(f32[3,2,32,1536]{3,2,0,1:T(8,128)} %copy-done.15) | copy-start | bytes 3538948
where the time goes:
time: 223 us; the launch traced here: 222 us
  blocking collectives  107 us (48%)
  local copies, waits for them, and re-layouts  43.2 us (19%)
  starting transfers between devices  38.4 us (17%)
  other arithmetic  17 us (8%)
  matrix products  15.1 us (7%)
    psum x1, blocking collectives, per_device(): filter_grad = lax.psum(local_grad, ('patch', 'map')) * scale  107 us
    ppermute x4, starting transfers between devices, extended_2(): lax.ppermute(head, axis, [((i + 1) % count, i) for i in range(count)])  26.1 us
    ppermute x4, starting transfers between devices, extended_2(): lax.ppermute(tail, axis, [(i, (i + 1) % count) for i in range(count)])  12.2 us
    another operation x4, local copies, waits for them, and re-layouts  6 us
    dot_general x2, matrix products, offset_sums(): jnp.einsum('uje,nujq->nueq', offset_mask.astype(jnp.float32), contrib, pr...  4.57 us
    convert_element_type x3, local copies, waits for them, and re-layouts, per_device(): x_one = forward_apply(maps).astype(jnp.bfloat16)  4.53 us
  transfers between devices with their start and end apart: 8, of which 0 were waited for; matrix products, arithmetic and copies ran while one was open for 17% of the time, Pallas kernels for 0%

commit v1 on v0

--- a/solution.py
+++ b/solution.py
@@ -100,7 +100,7 @@
     )
     scale = 1.0 / math.sqrt(map_count * lax.axis_size("map") * pix_count * patch_count)
     local_grad = jnp.einsum("kmcp,mop->kco", terms, cotangent, preferred_element_type=jnp.float32)
-    filter_grad = lax.psum(local_grad, ("patch", "map")) * scale
+    filter_grad = lax.psum(lax.psum(local_grad, "patch"), "map") * scale
     return (output, input_grad, filter_grad)
 
 

time: 223 us -> 310 us (1.39)
  the two profiles are of different devices: /device:TPU:1 before, /device:TPU:2 now
where the time goes in v1:
time: 310 us; the launch traced here: 309 us
  blocking collectives  195 us (63%)
  local copies, waits for them, and re-layouts  43.3 us (14%)
  starting transfers between devices  36.8 us (12%)
  other arithmetic  17 us (5%)
  matrix products  15.1 us (5%)
    psum x2, blocking collectives, per_device(): filter_grad = lax.psum(lax.psum(local_grad, 'patch'), 'map') * scale  195 us
    ppermute x4, starting transfers between devices, extended_2(): lax.ppermute(head, axis, [((i + 1) % count, i) for i in range(count)])  29.2 us
    ppermute x4, starting transfers between devices, extended_2(): lax.ppermute(tail, axis, [(i, (i + 1) % count) for i in range(count)])  7.64 us
  transfers between devices with their start and end apart: 8, of which 0 were waited for; matrix products, arithmetic and copies ran while one was open for 12% of the time, Pallas kernels for 0%

profile of v1, /device:TPU:2, one launch (start us, length us, event | category | flops | bytes accessed | tf_op | source)
XLA Modules:
  0.0 308.6 jit_solution(4678187027366399584)
XLA Ops:
  4.6 2.3 convolution_bitcast_fusion.3
  6.9 1.8 fusion.56
  10.8 1.8 reshape.181
  12.6 1.8 fusion.58
  14.4 1.9 collective-permute-start.4
  16.3 7.3 %collective-permute-start.5 = (f32[2,32,512]{2,1,0:T(8,128)}, f32[2,32,512]{2,1,0:T(8,128)}, u32[]{:S(2)}, u32[]{:S(2)}) collective-permute-start(f32[2,32,512]{2,1,0:T(8,128)} %get-tuple-element.67), channel_id=1, source_target_pairs={{32,0},{64,32},{96,64},{128,96},{160,128},{192,160},{224,192},{256... | collective-permute-start | bytes 393224 | tf_op jit(solution)/shard_map/ppermute | solution.py:19
  25.1 1.9 collective-permute-start
  27.0 7.3 %collective-permute-start.1 = (bf16[2,32,512]{2,1,0:T(8,128)(2,1)}, bf16[2,32,512]{2,1,0:T(8,128)(2,1)}, u32[]{:S(2)}, u32[]{:S(2)}) collective-permute-start(bf16[2,32,512]{2,1,0:T(8,128)(2,1)} %get-tuple-element.72), channel_id=1, source_target_pairs={{32,0},{64,32},{96,64},{128,96},{160,128},{192,160},{224,192},{256... | collective-permute-start | bytes 196616 | tf_op jit(solution)/shard_map/ppermute | solution.py:19
  34.3 1.8 slice.264
  37.0 1.9 squeeze.35
  45.0 1.9 convert_element_type.73
  46.9 1.9 convert_element_type.72
  50.3 1.9 collective-permute-start.2
  52.2 7.4 %collective-permute-start.3 = (bf16[2,32,512]{2,1,0:T(8,128)(2,1)}, bf16[2,32,512]{2,1,0:T(8,128)(2,1)}, u32[]{:S(2)}, u32[]{:S(2)}) collective-permute-start(bf16[2,32,512]{2,1,0:T(8,128)(2,1)} %get-tuple-element.70), channel_id=1, source_target_pairs={{32,0},{64,32},{96,64},{128,96},{160,128},{192,160},{224,192},{256... | collective-permute-start | bytes 196616 | tf_op jit(solution)/shard_map/ppermute | solution.py:19
  59.7 1.7 reshape.182
  61.3 1.7 fusion.44
  67.2 2.3 convolution_bitcast_fusion.2
  69.5 1.8 fusion.55
  81.3 2.0 convolution_bitcast_fusion.6
  85.1 1.9 reshape.184
  87.0 1.7 fusion.57
  88.7 1.9 collective-permute-start.6
  90.6 1.8 slice.279
  92.4 7.2 %collective-permute-start.7 = (f32[2,32,512]{2,1,0:T(8,128)}, f32[2,32,512]{2,1,0:T(8,128)}, u32[]{:S(2)}, u32[]{:S(2)}) collective-permute-start(f32[2,32,512]{2,1,0:T(8,128)} %get-tuple-element.65), channel_id=1, source_target_pairs={{32,0},{64,32},{96,64},{128,96},{160,128},{192,160},{224,192},{256... | collective-permute-start | bytes 393224 | tf_op jit(solution)/shard_map/ppermute | solution.py:19
  99.6 66.2 %psum.14 = f32[3,32,32]{2,1,0:T(8,128)} all-reduce(f32[3,32,32]{2,1,0:T(8,128)} %convolution_bitcast_fusion.6), channel_id=1, replica_groups=mesh['patch'=16,'map'=32] {'patch'}, use_global_device_ids=true, to_apply=%region_0.1 | all-reduce | flops 3072 | bytes 24576 | tf_op jit(solution)/shard_map/psum | solution.py:103
  165.8 128.9 %psum.15 = f32[3,32,32]{2,1,0:T(8,128)} all-reduce(f32[3,32,32]{2,1,0:T(8,128)} %psum.14), channel_id=1, replica_groups=mesh['patch'=16,'map'=32] {'map'}, use_global_device_ids=true, to_apply=%region_1.2 | all-reduce | flops 3072 | bytes 24576 | tf_op jit(solution)/shard_map/psum | solution.py:103
  296.2 1.7 reshape.185
  297.8 1.7 fusion.42
  299.5 1.7 reshape.186
  302.9 2.0 copy.42
  304.9 1.9 reshape.187
  306.8 1.7 fusion.20
  (110 shorter events, 34.9 us)
Async XLA Ops:
  0.6 3.5 %copy-start = (bf16[6,3,256,256]{3,2,1,0:T(8,128)(2,1)S(1)}, bf16[6,3,256,256]{3,2,1,0:T(8,128)(2,1)}, u32[]{:S(2)}) copy-start(bf16[6,3,256,256]{3,2,1,0:T(8,128)(2,1)} %param.15) | copy-start | bytes 7077892
  2.8 1.0 copy-start.15
  8.8 27.2 %copy-start.7 = (f32[64,6,256]{2,0,1:T(8,128)}, f32[64,6,256]{2,0,1:T(8,128)S(1)}, u32[]{:S(2)}) copy-start(f32[64,6,256]{2,0,1:T(8,128)S(1)} %get-tuple-element.73) | copy-start | bytes 1179652
  8.9 27.2 %copy-start.9 = (f32[64,6,256]{2,0,1:T(8,128)}, f32[64,6,256]{2,0,1:T(8,128)S(1)}, u32[]{:S(2)}) copy-start(f32[64,6,256]{2,0,1:T(8,128)S(1)} %get-tuple-element.74) | copy-start | bytes 1179652
  8.9 0.9 copy-start.11
  8.9 0.9 copy-start.13
  12.6 23.5 %copy-start.12 = (f32[64,6,256]{2,0,1:T(8,128)S(1)}, f32[64,6,256]{2,0,1:T(8,128)}, u32[]{:S(2)}) copy-start(f32[64,6,256]{2,0,1:T(8,128)} %copy-done.11) | copy-start | bytes 1179652
  12.6 23.5 %copy-start.14 = (f32[64,6,256]{2,0,1:T(8,128)S(1)}, f32[64,6,256]{2,0,1:T(8,128)}, u32[]{:S(2)}) copy-start(f32[64,6,256]{2,0,1:T(8,128)} %copy-done.13) | copy-start | bytes 1179652
  14.4 45.3 %collective-permute-start.4 = (f32[2,32,512]{2,1,0:T(8,128)}, f32[2,32,512]{2,1,0:T(8,128)}, u32[]{:S(2)}, u32[]{:S(2)}) collective-permute-start(f32[2,32,512]{2,1,0:T(8,128)} %get-tuple-element.68), channel_id=1, source_target_pairs={{0,32},{32,64},{64,96},{96,128},{128,160},{160,192},{192,224},{224... | collective-permute-start | bytes 393224 | tf_op jit(solution)/shard_map/ppermute | solution.py:17
  16.3 46.7 %collective-permute-start.5 = (f32[2,32,512]{2,1,0:T(8,128)}, f32[2,32,512]{2,1,0:T(8,128)}, u32[]{:S(2)}, u32[]{:S(2)}) collective-permute-start(f32[2,32,512]{2,1,0:T(8,128)} %get-tuple-element.67), channel_id=1, source_target_pairs={{32,0},{64,32},{96,64},{128,96},{160,128},{192,160},{224,192},{256... | collective-permute-start | bytes 393224 | tf_op jit(solution)/shard_map/ppermute | solution.py:19
  25.1 13.8 %collective-permute-start = (bf16[2,32,512]{2,1,0:T(8,128)(2,1)}, bf16[2,32,512]{2,1,0:T(8,128)(2,1)}, u32[]{:S(2)}, u32[]{:S(2)}) collective-permute-start(bf16[2,32,512]{2,1,0:T(8,128)(2,1)} %get-tuple-element.71), channel_id=1, source_target_pairs={{0,32},{32,64},{64,96},{96,128},{128,160},{160,192},{192,224},{224... | collective-permute-start | bytes 196616 | tf_op jit(solution)/shard_map/ppermute | solution.py:17
  27.0 11.9 %collective-permute-start.1 = (bf16[2,32,512]{2,1,0:T(8,128)(2,1)}, bf16[2,32,512]{2,1,0:T(8,128)(2,1)}, u32[]{:S(2)}, u32[]{:S(2)}) collective-permute-start(bf16[2,32,512]{2,1,0:T(8,128)(2,1)} %get-tuple-element.72), channel_id=1, source_target_pairs={{32,0},{64,32},{96,64},{128,96},{160,128},{192,160},{224,192},{256... | collective-permute-start | bytes 196616 | tf_op jit(solution)/shard_map/ppermute | solution.py:19
  36.2 2.7 copy-start.18
  44.2 17.1 %copy-start.8 = (f32[64,6,256]{2,0,1:T(8,128)S(1)}, f32[64,6,256]{2,0,1:T(8,128)}, u32[]{:S(2)}) copy-start(f32[64,6,256]{2,0,1:T(8,128)} %copy-done.7) | copy-start | bytes 1179652
  44.2 17.1 %copy-start.10 = (f32[64,6,256]{2,0,1:T(8,128)S(1)}, f32[64,6,256]{2,0,1:T(8,128)}, u32[]{:S(2)}) copy-start(f32[64,6,256]{2,0,1:T(8,128)} %copy-done.9) | copy-start | bytes 1179652
  50.3 23.2 %collective-permute-start.2 = (bf16[2,32,512]{2,1,0:T(8,128)(2,1)}, bf16[2,32,512]{2,1,0:T(8,128)(2,1)}, u32[]{:S(2)}, u32[]{:S(2)}) collective-permute-start(bf16[2,32,512]{2,1,0:T(8,128)(2,1)} %get-tuple-element.69), channel_id=1, source_target_pairs={{0,32},{32,64},{64,96},{96,128},{128,160},{160,192},{192,224},{224... | collective-permute-start | bytes 196616 | tf_op jit(solution)/shard_map/ppermute | solution.py:17
  52.2 21.3 %collective-permute-start.3 = (bf16[2,32,512]{2,1,0:T(8,128)(2,1)}, bf16[2,32,512]{2,1,0:T(8,128)(2,1)}, u32[]{:S(2)}, u32[]{:S(2)}) collective-permute-start(bf16[2,32,512]{2,1,0:T(8,128)(2,1)} %get-tuple-element.70), channel_id=1, source_target_pairs={{32,0},{64,32},{96,64},{128,96},{160,128},{192,160},{224,192},{256... | collective-permute-start | bytes 196616 | tf_op jit(solution)/shard_map/ppermute | solution.py:19
  71.4 1.3 copy-start.1
  71.5 1.3 copy-start.3
  71.5 1.2 copy-start.5
  71.6 1.2 copy-start.6
  72.8 1.0 copy-start.17
  79.1 1.1 copy-start.19
  80.2 3.1 copy-start.22
  80.2 3.1 copy-start.23
  81.3 3.0 copy-start.20
  81.3 2.9 copy-start.21
  85.1 212.7 %copy-start.2 = (f32[64,6,1,256]{3,0,1,2:T(8,128)S(1)}, f32[64,6,1,256]{3,0,1,2:T(8,128)}, u32[]{:S(2)}) copy-start(f32[64,6,1,256]{3,0,1,2:T(8,128)} %copy-done.1) | copy-start | bytes 1179652
  85.1 212.7 %copy-start.4 = (f32[64,6,1,256]{3,0,1,2:T(8,128)S(1)}, f32[64,6,1,256]{3,0,1,2:T(8,128)}, u32[]{:S(2)}) copy-start(f32[64,6,1,256]{3,0,1,2:T(8,128)} %copy-done.3) | copy-start | bytes 1179652
  88.7 207.5 %collective-permute-start.6 = (f32[2,32,512]{2,1,0:T(8,128)}, f32[2,32,512]{2,1,0:T(8,128)}, u32[]{:S(2)}, u32[]{:S(2)}) collective-permute-start(f32[2,32,512]{2,1,0:T(8,128)} %get-tuple-element.66), channel_id=1, source_target_pairs={{0,32},{32,64},{64,96},{96,128},{128,160},{160,192},{192,224},{224... | collective-permute-start | bytes 393224 | tf_op jit(solution)/shard_map/ppermute | solution.py:17
  92.4 207.1 %collective-permute-start.7 = (f32[2,32,512]{2,1,0:T(8,128)}, f32[2,32,512]{2,1,0:T(8,128)}, u32[]{:S(2)}, u32[]{:S(2)}) collective-permute-start(f32[2,32,512]{2,1,0:T(8,128)} %get-tuple-element.65), channel_id=1, source_target_pairs={{32,0},{64,32},{96,64},{128,96},{160,128},{192,160},{224,192},{256... | collective-permute-start | bytes 393224 | tf_op jit(solution)/shard_map/ppermute | solution.py:19
  299.5 7.3 %copy-start.16 = (f32[3,2,32,1536]{3,2,0,1:T(8,128)S(1)}, f32[3,2,32,1536]{3,2,0,1:T(8,128)}, u32[]{:S(2)}) copy-start(f32[3,2,32,1536]{3,2,0,1:T(8,128)} %copy-done.15) | copy-start | bytes 3538948
